TPU v7x, 32 devices: a whole 2x2x4 slice. The times are simulated.
32 devices in a mesh: group: 4 (over z), member: 8 (over y, x, core).
Axes of the slice: x: 2, y: 2, z: 4, core: 2. Of those that a mesh axis runs over, the one named last changes fastest.
Arguments:
- query_feat: bfloat16 [4096, 4096], P(('group', 'member'))
- code_feat: bfloat16 [4096, 4096], P(('group', 'member'))
- projection: bfloat16 [4096, 1024], replicated
- hard_ids: int32 [32, 16], P(('group', 'member')), may hold values from 0 to 63, as said below
- loss_weight: float32 [4096], P(('group', 'member')), may hold values from 1 to 4
Outputs:
- query_grad: bfloat16 [4096, 4096], P(('group', 'member'))
- code_grad: bfloat16 [4096, 4096], P(('group', 'member'))
- projection_grad: float32 [4096, 1024], P(('group', 'member'))
Inputs may be any that keep to these rules, and one draw needn't show every extreme that they name: `hard_ids`: entry (owner device g * 8 + m) * 2 + slot names code rows of that device. A row names 16 different blocks, none of its own group; at most 8 of them lie in one group, and exactly 8 in some group of every row.
All inputs are finite; a program needn't handle non-finite values.
Results may differ from a plain program's by a relative error of at most 0.02.
Values may be sent and summed in bfloat16 or wider, within the bound.
No kernel may reach another device: no remote copies, remote signals or barrier semaphores. Data moves between devices by JAX's collectives and lax.ppermute only.
A program may use at most 128 MiB of HBM per device.

v0:
```python
import jax
import jax.numpy as jnp
from jax import lax
from jax.sharding import PartitionSpec as P

CB = 64
inverse_temp = 120.0
epsilon = 1e-06


def embed(features, projection):
    values = jnp.dot(features, projection, preferred_element_type=jnp.float32)
    inverse = lax.rsqrt(jnp.sum(values * values, axis=1) + epsilon)
    unit_vec = values * inverse[:, None]
    return (unit_vec, inverse, unit_vec.astype(jnp.bfloat16))


def norm_back(upstream, unit_vec, inverse):
    inner_prod = jnp.sum(unit_vec * upstream, axis=1, keepdims=True)
    return (inverse[:, None] * (upstream - unit_vec * inner_prod)).astype(jnp.bfloat16)


def shift_all(x, axis):
    size = lax.axis_size(axis)
    index = lax.axis_index(axis)
    got = [x]
    for s in range(1, size):
        got.append(lax.ppermute(x, axis, [(i, (i + s) % size) for i in range(size)]))
    order = (index - jnp.arange(size)) % size
    return jax.tree.map(lambda *xs: jnp.take(jnp.stack(xs, axis=0), order, axis=0), *got)


def exchange(parts, axis):
    size = lax.axis_size(axis)
    index = lax.axis_index(axis)
    got = [jnp.take(parts, index, axis=0)]
    for s in range(1, size):
        sent = jnp.take(parts, (index + s) % size, axis=0)
        got.append(lax.ppermute(sent, axis, [(i, (i + s) % size) for i in range(size)]))
    stacked = jnp.stack(got, axis=0)
    return jnp.take(stacked, (index - jnp.arange(size)) % size, axis=0)


def body(query_feat, code_feat, projection, hard_ids, loss_weight):
    groups = lax.axis_size("group")
    members = lax.axis_size("member")
    group_index = lax.axis_index("group")
    member_index = lax.axis_index("member")
    queries_dev = query_feat.shape[0]
    feat_width = query_feat.shape[1]
    emb_width = projection.shape[1]
    slot_count = queries_dev // CB
    per_group = members * slot_count
    group_span = members * queries_dev
    rows_dev = feat_width // (groups * members)
    feats = jnp.stack([query_feat, code_feat], axis=0).reshape(
        2, queries_dev, groups, members, rows_dev
    )
    feats = jnp.transpose(feats, (3, 0, 1, 2, 4))
    feat_cols = lax.all_to_all(feats, "member", split_axis=0, concat_axis=0, tiled=True)
    q_unit, q_inv, q_emb = embed(query_feat, projection)
    code_values = lax.all_gather(
        jnp.dot(code_feat, projection, preferred_element_type=jnp.float32),
        "member",
        axis=0,
        tiled=True,
    )
    c_inv = lax.rsqrt(jnp.sum(code_values * code_values, axis=1) + epsilon)
    c_unit = code_values * c_inv[:, None]
    group_codes = c_unit.astype(jnp.bfloat16)
    q_all = lax.all_to_all(
        jnp.broadcast_to(q_emb[None], (groups, queries_dev, emb_width)),
        "group",
        split_axis=0,
        concat_axis=0,
        tiled=True,
    )
    ids_all = shift_all(hard_ids[0], "group")
    block_ids = group_index * per_group + jnp.arange(per_group, dtype=jnp.int32)
    asked = jnp.any(ids_all[:, :, None] == block_ids[None, None, :], axis=1)
    own = jnp.arange(groups, dtype=jnp.int32) == group_index
    block_mask = asked | own[:, None]
    col_mask = jnp.broadcast_to(block_mask[:, :, None], (groups, per_group, CB)).reshape(
        groups, 1, group_span
    )
    scores = inverse_temp * jnp.einsum(
        "gqe,ke->gqk", q_all, group_codes, preferred_element_type=jnp.float32
    )
    scores = jnp.where(col_mask, scores, -jnp.inf)
    part_max = jnp.max(scores, axis=2)
    safe_max = jnp.where(part_max > -jnp.inf, part_max, 0.0)
    part_sum = jnp.sum(jnp.exp(scores - safe_max[:, :, None]), axis=2)
    weights_row = jnp.broadcast_to(loss_weight[None], (groups, queries_dev))
    stats = shift_all(jnp.stack([part_max, part_sum, weights_row], axis=0), "group")
    w_all = stats[:, 2, 0]
    row_max = jnp.max(stats[:, 0], axis=0)
    row_sum = jnp.sum(stats[:, 1] * jnp.exp(stats[:, 0] - row_max[None]), axis=0)
    log_total = row_max + jnp.log(row_sum)
    offsets = jnp.arange(queries_dev, dtype=jnp.int32)
    columns = jnp.arange(group_span, dtype=jnp.int32)
    positive = (columns[None, :] == (member_index * queries_dev + offsets)[:, None]).astype(
        jnp.float32
    )
    positive = positive[None] * own[:, None, None].astype(jnp.float32)
    factor = w_all * inverse_temp
    grad = (factor[:, :, None] * (jnp.exp(scores - log_total[:, :, None]) - positive)).astype(
        jnp.bfloat16
    )
    code_terms = None
    for g in range(groups):
        term = jnp.dot(grad[g].T, q_all[g], preferred_element_type=jnp.float32)
        term = jnp.where(g == group_index, term, term.astype(jnp.bfloat16).astype(jnp.float32))
        code_terms = term if code_terms is None else code_terms + term
    code_sum = code_terms.astype(jnp.bfloat16)
    grad_dq, code_sum = lax.optimization_barrier((grad, code_sum))
    code_delta = lax.psum(code_sum, "member").astype(jnp.float32)
    delta_parts = jnp.einsum(
        "gqk,ke->gqe", grad_dq, group_codes, preferred_element_type=jnp.float32
    )
    returned = exchange(delta_parts.astype(jnp.bfloat16), "group").astype(jnp.float32)
    own_part = jnp.take(delta_parts, group_index, axis=0)
    query_delta = own_part + jnp.sum(jnp.where(own[:, None, None], 0.0, returned), axis=0)
    dz_query = norm_back(query_delta, q_unit, q_inv)
    dz_code_all = norm_back(code_delta, c_unit, c_inv)
    dz_code = lax.dynamic_slice_in_dim(dz_code_all, member_index * queries_dev, queries_dev, 0)
    query_grad = jnp.einsum(
        "qe,de->qd", dz_query, projection, preferred_element_type=jnp.float32
    ).astype(jnp.bfloat16)
    code_grad = jnp.einsum(
        "qe,de->qd", dz_code, projection, preferred_element_type=jnp.float32
    ).astype(jnp.bfloat16)
    dzq_all = lax.all_to_all(
        jnp.broadcast_to(dz_query[None], (members, queries_dev, emb_width)),
        "member",
        split_axis=0,
        concat_axis=0,
        tiled=True,
    )
    dzc_all = dz_code_all.reshape(members, queries_dev, emb_width)
    proj_parts = jnp.einsum(
        "mqgr,mqe->gre", feat_cols[:, 0], dzq_all, preferred_element_type=jnp.float32
    ) + jnp.einsum("mqgr,mqe->gre", feat_cols[:, 1], dzc_all, preferred_element_type=jnp.float32)
    own_proj = jnp.take(proj_parts, group_index, axis=0)
    sent_proj = jnp.where(own[:, None, None], 0.0, proj_parts).astype(jnp.bfloat16)
    projection_grad = own_proj + lax.psum_scatter(
        sent_proj, "group", scatter_dimension=0, tiled=True
    ).reshape(rows_dev, emb_width).astype(jnp.float32)
    return (query_grad, code_grad, projection_grad)


def solution(mesh):
    return jax.shard_map(
        body,
        mesh=mesh,
        in_specs=(
            P(("group", "member"), None),
            P(("group", "member"), None),
            P(),
            P(("group", "member"), None),
            P(("group", "member")),
        ),
        out_specs=(
            P(("group", "member"), None),
            P(("group", "member"), None),
            P(("group", "member"), None),
        ),
        check_vma=False,
    )
```

profile of v0, /device:TPU:0, one launch (start us, length us, event | category | flops | bytes accessed | tf_op | source)
XLA Modules:
  0.0 204.6 jit_solution(2245639925189366476)
XLA Ops:
  7.2 5.8 %fusion.26 = f32[128,1024]{1,0:T(8,128)} fusion(bf16[128,4096]{1,0:T(8,128)(2,1)} %param.10, bf16[4096,1024]{1,0:T(8,128)(2,1)} %param.11), kind=kOutput, calls=%fused_computation.91 | convolution fusion | flops 1073741824 | bytes 9961472 | tf_op jit(solution)/shard_map/dot_general | solution.py:63
  13.1 3.1 %collective-permute-start = (s32[16]{0:T(128)S(1)}, s32[16]{0:T(128)S(1)}, u32[]{:S(2)}, u32[]{:S(2)}) collective-permute-start(s32[16]{0:T(128)S(1)} %bitcast.128), channel_id=1, source_target_pairs={{0,8},{8,16},{16,24},{24,0},{1,9},{9,17},{17,25},{25,1},{2,10},{10... | collective-permute-start | bytes 200 | tf_op jit(solution)/shard_map/ppermute | solution.py:28
  16.2 2.6 %collective-permute-start.1 = (s32[16]{0:T(128)S(1)}, s32[16]{0:T(128)S(1)}, u32[]{:S(2)}, u32[]{:S(2)}) collective-permute-start(s32[16]{0:T(128)S(1)} %bitcast.129), channel_id=1, source_target_pairs={{0,16},{8,24},{16,0},{24,8},{1,17},{9,25},{17,1},{25,9},{2,18},{10... | collective-permute-start | bytes 200 | tf_op jit(solution)/shard_map/ppermute | solution.py:28
  20.2 5.0 %multiply_reduce_fusion.2 = (f32[128]{0:T(128)S(1)}, f32[128,1024]{1,0:T(8,128)S(1)}) fusion(bf16[128,4096]{1,0:T(8,128)(2,1)S(1)} %copy-done.5, bf16[4096,1024]{1,0:T(8,128)(2,1)} %param.11), kind=kOutput, calls=%fused_computation.31 | convolution fusion | flops 1074003840 | bytes 9961984 | tf_op jit(solution)/shard_map/dot_general | solution.py:12
  26.4 3.6 %all-to-all-start = ((bf16[4,128,1024]{2,1,0:T(8,128)(2,1)}), bf16[4,128,1024]{2,1,0:T(8,128)(2,1)S(1)}, u32[]{:S(2)}, u32[]{:S(2)}) async-start(bf16[4,128,1024]{2,1,0:T(8,128)(2,1)} %broadcast_in_dim.126), calls=%async_computation | async-start | bytes 2097152 | tf_op jit(solution)/shard_map/all_to_all | solution.py:71
  37.5 15.0 %all-gather.2.cloned.1.call-done = f32[1024,1024]{1,0:T(8,128)} async-done(((f32[128,1024]{1,0:T(8,128)}), f32[1024,1024]{1,0:T(8,128)}) %all-gather.2.cloned.1.call-update) | async-done | bytes 4194320 | tf_op jit(solution)/shard_map/all_gather | solution.py:62
  52.6 2.5 %multiply_reduce_fusion = f32[1024]{0:T(1024)S(1)} fusion(f32[1024,1024]{1,0:T(8,128)} %all-gather.2.cloned.1.call-done), kind=kLoop, calls=%fused_computation.11 | loop fusion | flops 2096128 | bytes 4198400 | tf_op jit(solution)/shard_map/reduce_sum | solution.py:68
  55.1 4.4 %all-to-all-start.1 = ((bf16[8,2,128,4,128]{2,4,3,1,0:T(8,128)(2,1)}), bf16[8,2,128,4,128]{2,4,3,1,0:T(8,128)(2,1)}, u32[]{:S(2)}, u32[]{:S(2)}) async-start(bf16[8,2,128,4,128]{2,4,3,1,0:T(8,128)(2,1)} %copy.25), calls=%async_computation.1 | async-start | bytes 4194304 | tf_op jit(solution)/shard_map/all_to_all | solution.py:60
  59.5 3.6 %fusion.24 = (f32[4,128]{1,0:T(4,128)S(1)}, f32[4,128,1024]{2,1,0:T(8,128)S(1)}) fusion(bf16[4,128,1024]{2,1,0:T(8,128)(2,1)S(1)} %all-to-all-done, f32[1024,1024]{1,0:T(8,128)} %all-gather.2.cloned.1.call-done, f32[1024]{0:T(1024)S(1)} %add_rsqrt_fusion, pred[4,1024]{1,0:T(4,128)(4,1)S(1)} %broadcast_in_dim.124), kind=kOutput, calls=%fused_computation.89 | convolution fusion | flops 1077411328 | bytes 7350272 | tf_op jit(solution)/shard_map/gqe,ke->gqk/dot_general | solution.py:86
  69.9 3.2 %collective-permute-done.3 = f32[3,4,128]{2,1,0:T(4,128)S(1)} collective-permute-done((f32[3,4,128]{2,1,0:T(4,128)S(1)}, f32[3,4,128]{2,1,0:T(4,128)S(1)}, u32[]{:S(2)}, u32[]{:S(2)}) %collective-permute-start.3) | collective-permute-done | bytes 6176 | tf_op jit(solution)/shard_map/ppermute | solution.py:28
  80.1 3.8 %fusion.25 = (bf16[4,128,1024]{2,1,0:T(8,128)(2,1)S(1)}, f32[4,128,1024]{2,1,0:T(8,128)S(1)}) fusion(bf16[4,128,1024]{2,1,0:T(8,128)(2,1)} %copy-done.1, f32[1024,1024]{1,0:T(8,128)} %all-gather.2.cloned.1.call-done, f32[1024]{0:T(1024)S(1)} %add_rsqrt_fusion), kind=kOutput, calls=%fused_computation.90 | convolution fusion | flops 1076363264 | bytes 8392704 | tf_op jit(solution)/shard_map/gqk,ke->gqe/dot_general | solution.py:117
  85.4 3.3 %collective-permute-start.8 = (bf16[128,1024]{1,0:T(8,128)(2,1)}, bf16[128,1024]{1,0:T(8,128)(2,1)S(1)}, u32[]{:S(2)}, u32[]{:S(2)}) collective-permute-start(bf16[128,1024]{1,0:T(8,128)(2,1)} %get-tuple-element.34), channel_id=1, source_target_pairs={{0,24},{8,0},{16,8},{24,16},{1,25},{9,1},{17,9},{25,17},{2,26},{10... | collective-permute-start | bytes 786440 | tf_op jit(solution)/shard_map/ppermute | solution.py:39
  88.7 7.4 %collective-permute-done.6 = bf16[128,1024]{1,0:T(8,128)(2,1)S(1)} collective-permute-done((bf16[128,1024]{1,0:T(8,128)(2,1)}, bf16[128,1024]{1,0:T(8,128)(2,1)S(1)}, u32[]{:S(2)}, u32[]{:S(2)}) %collective-permute-start.6) | collective-permute-done | bytes 262176 | tf_op jit(solution)/shard_map/ppermute | solution.py:39
  96.2 8.9 %collective-permute-done.7 = bf16[128,1024]{1,0:T(8,128)(2,1)S(1)} collective-permute-done((bf16[128,1024]{1,0:T(8,128)(2,1)}, bf16[128,1024]{1,0:T(8,128)(2,1)S(1)}, u32[]{:S(2)}, u32[]{:S(2)}) %collective-permute-start.7) | collective-permute-done | bytes 262176 | tf_op jit(solution)/shard_map/ppermute | solution.py:39
  106.2 2.9 %gather_fusion.2 = bf16[4,128,1024]{2,1,0:T(8,128)(2,1)} fusion(bf16[4,128,1024]{2,1,0:T(8,128)(2,1)} %pad_maximum_fusion, s32[1024]{0:T(1024)S(1)} %pad_clamp_fusion), kind=kCustom, calls=%fused_computation.2 | custom fusion | bytes 2097168 | tf_op jit(solution)/shard_map/jit(_take)/gather | solution.py:41
  112.7 4.3 %all-to-all-start.2 = ((bf16[8,128,1024]{2,1,0:T(8,128)(2,1)}), bf16[8,128,1024]{2,1,0:T(8,128)(2,1)}, u32[]{:S(2)}, u32[]{:S(2)}) async-start(bf16[8,128,1024]{2,1,0:T(8,128)(2,1)} %broadcast_in_dim.134), calls=%async_computation.2 | async-start | bytes 4194304 | tf_op jit(solution)/shard_map/all_to_all | solution.py:132
  117.1 2.8 %fusion.23 = (bf16[8,1,128,4,128]{2,4,3,1,0:T(8,128)(2,1)S(1)}, bf16[8,1,128,4,128]{2,4,3,1,0:T(8,128)(2,1)}) fusion(bf16[8,2,128,4,128]{2,4,3,1,0:T(8,128)(2,1)} %all-to-all-done.1), kind=kLoop, calls=%fused_computation.88 | loop fusion | bytes 4194304 | tf_op jit(solution)/shard_map/slice | solution.py:142
  119.9 37.8 %all-reduce.2.cloned.1.call-done = bf16[1024,1024]{1,0:T(8,128)(2,1)} async-done(((bf16[1024,1024]{1,0:T(8,128)(2,1)}), bf16[1024,1024]{1,0:T(8,128)(2,1)}) %all-reduce.2.cloned.1.call-update) | async-done | bytes 2097168 | tf_op jit(solution)/shard_map/psum | solution.py:116
  157.7 3.7 %fusion = f32[1024]{0:T(1024)S(1)} fusion(bf16[1024,1024]{1,0:T(8,128)(2,1)} %all-reduce.2.cloned.1.call-done, f32[1024,1024]{1,0:T(8,128)} %all-gather.2.cloned.1.call-done, f32[1024]{0:T(1024)S(1)} %add_rsqrt_fusion), kind=kLoop, calls=%fused_computation.7 | loop fusion | flops 4193280 | bytes 6299648 | tf_op jit(solution)/shard_map/reduce_sum | solution.py:19
  163.2 3.2 %fusion.4 = f32[4,128,1024,1]{2,1,3,0:T(8,128)S(1)} fusion(bf16[8,128,1024]{2,1,0:T(8,128)(2,1)} %all-to-all-done.2, bf16[8,1,128,4,128]{2,4,3,1,0:T(8,128)(2,1)} %get-tuple-element.32), kind=kOutput, calls=%fused_computation.16 | convolution fusion | flops 1073741824 | bytes 5242880 | tf_op jit(solution)/shard_map/mqgr,mqe->gre/dot_general | solution.py:140
  166.4 2.9 %select_convert_fusion = (bf16[4,128,1024]{2,1,0:T(8,128)(2,1)}, f32[4,128,1024]{2,1,0:T(8,128)}) fusion(pred[4]{0:T(512)(128)(4,1)S(1)} %iota_compare_fusion.1, bf16[8,128,1024,1]{2,1,0,3:T(8,128)(2,1)S(1)} %bitcast.116, bf16[8,1,128,4,128]{2,4,3,1,0:T(8,128)(2,1)S(1)} %get-tuple-element.31, f32[4,128,1024,1]{2,1,3,0:T(8,128)S(1)} %fusion.4), kind=kOutput, calls=%fused_computation.18 | convolution fusion | flops 1074790400 | bytes 8388612 | tf_op jit(solution)/shard_map/mqgr,mqe->gre/dot_general | solution.py:142
  169.3 7.2 %convolution_convert_fusion.1 = bf16[128,4096]{1,0:T(8,128)(2,1)} fusion(bf16[128,1024]{1,0:T(8,128)(2,1)S(1)} %multiply_convert_fusion.2, bf16[4096,1024]{1,0:T(8,128)(2,1)} %param.11), kind=kOutput, calls=%fused_computation.6 | convolution fusion | flops 1074266112 | bytes 9699328 | tf_op jit(solution)/shard_map/qe,de->qd/dot_general | solution.py:126
  176.6 7.2 %convolution_convert_fusion = bf16[128,4096]{1,0:T(8,128)(2,1)} fusion(bf16[4096,1024]{1,0:T(8,128)(2,1)} %param.11, bf16[1024,1024]{1,0:T(8,128)(2,1)S(1)} %fusion.2, s32[]{:T(128)S(6)} %select_n.153), kind=kOutput, calls=%fused_computation.5 | convolution fusion | flops 1074266112 | bytes 9699332 | tf_op jit(solution)/shard_map/qe,de->qd/dot_general | solution.py:129
  183.8 12.3 %reduce-scatter.2.cloned.1.call-done = bf16[1,128,1024]{2,1,0:T(8,128)(2,1)} async-done(((bf16[4,128,1024]{2,1,0:T(8,128)(2,1)}), bf16[1,128,1024]{2,1,0:T(8,128)(2,1)}) %reduce-scatter.2.cloned.1.call-update) | async-done | bytes 262160 | tf_op jit(solution)/shard_map/reduce_scatter | solution.py:145
  (88 shorter events, 33.8 us)
Async XLA Ops:
  7.2 5.9 %copy-start.9 = (s32[1,16]{1,0:T(1,128)S(1)}, s32[1,16]{1,0:T(1,128)}, u32[]{:S(2)}) copy-start(s32[1,16]{1,0:T(1,128)} %param.12) | copy-start | bytes 196
  7.2 13.0 %copy-start.5 = (bf16[128,4096]{1,0:T(8,128)(2,1)S(1)}, bf16[128,4096]{1,0:T(8,128)(2,1)}, u32[]{:S(2)}) copy-start(bf16[128,4096]{1,0:T(8,128)(2,1)} %param.9) | copy-start | bytes 3145732
  7.2 45.4 %all-gather.2.cloned.1.call-start = ((), (), s32[]{:S(2)}) async-start(), calls=%async_computation.4 | async-start | bytes 4718592 | tf_op jit(solution)/shard_map/all_gather | solution.py:62
  13.1 23.4 %collective-permute-start = (s32[16]{0:T(128)S(1)}, s32[16]{0:T(128)S(1)}, u32[]{:S(2)}, u32[]{:S(2)}) collective-permute-start(s32[16]{0:T(128)S(1)} %bitcast.128), channel_id=1, source_target_pairs={{0,8},{8,16},{16,24},{24,0},{1,9},{9,17},{17,25},{25,1},{2,10},{10... | collective-permute-start | bytes 200 | tf_op jit(solution)/shard_map/ppermute | solution.py:28
  16.2 20.3 %collective-permute-start.1 = (s32[16]{0:T(128)S(1)}, s32[16]{0:T(128)S(1)}, u32[]{:S(2)}, u32[]{:S(2)}) collective-permute-start(s32[16]{0:T(128)S(1)} %bitcast.129), channel_id=1, source_target_pairs={{0,16},{8,24},{16,0},{24,8},{1,17},{9,25},{17,1},{25,9},{2,18},{10... | collective-permute-start | bytes 200 | tf_op jit(solution)/shard_map/ppermute | solution.py:28
  18.8 17.7 %collective-permute-start.2 = (s32[16]{0:T(128)S(1)}, s32[16]{0:T(128)S(1)}, u32[]{:S(2)}, u32[]{:S(2)}) collective-permute-start(s32[16]{0:T(128)S(1)} %bitcast.130), channel_id=1, source_target_pairs={{0,24},{8,0},{16,8},{24,16},{1,25},{9,1},{17,9},{25,17},{2,26},{10... | collective-permute-start | bytes 200 | tf_op jit(solution)/shard_map/ppermute | solution.py:28
  25.1 1.2 copy-start.3
  26.4 5.1 %copy-start.6 = (bf16[128,4096]{1,0:T(8,128)(2,1)S(1)}, bf16[128,4096]{1,0:T(8,128)(2,1)}, u32[]{:S(2)}) copy-start(bf16[128,4096]{1,0:T(8,128)(2,1)} %param.10) | copy-start | bytes 3145732
  26.4 28.7 %all-to-all-start = ((bf16[4,128,1024]{2,1,0:T(8,128)(2,1)}), bf16[4,128,1024]{2,1,0:T(8,128)(2,1)S(1)}, u32[]{:S(2)}, u32[]{:S(2)}) async-start(bf16[4,128,1024]{2,1,0:T(8,128)(2,1)} %broadcast_in_dim.126), calls=%async_computation | async-start | bytes 2097152 | tf_op jit(solution)/shard_map/all_to_all | solution.py:71
  31.4 1.3 copy-start.7
  55.1 56.0 %all-to-all-start.1 = ((bf16[8,2,128,4,128]{2,4,3,1,0:T(8,128)(2,1)}), bf16[8,2,128,4,128]{2,4,3,1,0:T(8,128)(2,1)}, u32[]{:S(2)}, u32[]{:S(2)}) async-start(bf16[8,2,128,4,128]{2,4,3,1,0:T(8,128)(2,1)} %copy.25), calls=%async_computation.1 | async-start | bytes 4194304 | tf_op jit(solution)/shard_map/all_to_all | solution.py:60
  59.5 98.2 %all-reduce.2.cloned.1.call-start = ((), (), s32[]{:S(2)}) async-start(), calls=%async_computation.5 | async-start | bytes 4194304 | tf_op jit(solution)/shard_map/psum | solution.py:116
  63.8 4.6 %collective-permute-start.4 = (f32[3,4,128]{2,1,0:T(4,128)S(1)}, f32[3,4,128]{2,1,0:T(4,128)S(1)}, u32[]{:S(2)}, u32[]{:S(2)}) collective-permute-start(f32[3,4,128]{2,1,0:T(4,128)S(1)} %get-tuple-element.38), channel_id=1, source_target_pairs={{0,16},{8,24},{16,0},{24,8},{1,17},{9,25},{17,1},{25,9},{2,18},{10... | collective-permute-start | bytes 18440 | tf_op jit(solution)/shard_map/ppermute | solution.py:28
  66.3 3.6 %collective-permute-start.5 = (f32[3,4,128]{2,1,0:T(4,128)S(1)}, f32[3,4,128]{2,1,0:T(4,128)S(1)}, u32[]{:S(2)}, u32[]{:S(2)}) collective-permute-start(f32[3,4,128]{2,1,0:T(4,128)S(1)} %get-tuple-element.38), channel_id=1, source_target_pairs={{0,24},{8,0},{16,8},{24,16},{1,25},{9,1},{17,9},{25,17},{2,26},{10... | collective-permute-start | bytes 18440 | tf_op jit(solution)/shard_map/ppermute | solution.py:28
  67.7 5.4 %collective-permute-start.3 = (f32[3,4,128]{2,1,0:T(4,128)S(1)}, f32[3,4,128]{2,1,0:T(4,128)S(1)}, u32[]{:S(2)}, u32[]{:S(2)}) collective-permute-start(f32[3,4,128]{2,1,0:T(4,128)S(1)} %get-tuple-element.38), channel_id=1, source_target_pairs={{0,8},{8,16},{16,24},{24,0},{1,9},{9,17},{17,25},{25,1},{2,10},{10... | collective-permute-start | bytes 18440 | tf_op jit(solution)/shard_map/ppermute | solution.py:28
  75.5 2.2 %copy-start.1 = (bf16[4,128,1024]{2,1,0:T(8,128)(2,1)}, bf16[4,128,1024]{2,1,0:T(8,128)(2,1)S(1)}, u32[]{:S(2)}) copy-start(bf16[4,128,1024]{2,1,0:T(8,128)(2,1)S(1)} %multiply_convert_fusion.1) | copy-start | bytes 3145732
  84.9 11.3 %collective-permute-start.6 = (bf16[128,1024]{1,0:T(8,128)(2,1)}, bf16[128,1024]{1,0:T(8,128)(2,1)S(1)}, u32[]{:S(2)}, u32[]{:S(2)}) collective-permute-start(bf16[128,1024]{1,0:T(8,128)(2,1)} %get-tuple-element.36), channel_id=1, source_target_pairs={{0,8},{8,16},{16,24},{24,0},{1,9},{9,17},{17,25},{25,1},{2,10},{10... | collective-permute-start | bytes 786440 | tf_op jit(solution)/shard_map/ppermute | solution.py:39
  84.9 20.2 %collective-permute-start.7 = (bf16[128,1024]{1,0:T(8,128)(2,1)}, bf16[128,1024]{1,0:T(8,128)(2,1)S(1)}, u32[]{:S(2)}, u32[]{:S(2)}) collective-permute-start(bf16[128,1024]{1,0:T(8,128)(2,1)} %get-tuple-element.35), channel_id=1, source_target_pairs={{0,16},{8,24},{16,0},{24,8},{1,17},{9,25},{17,1},{25,9},{2,18},{10... | collective-permute-start | bytes 786440 | tf_op jit(solution)/shard_map/ppermute | solution.py:39
  85.4 19.6 %collective-permute-start.8 = (bf16[128,1024]{1,0:T(8,128)(2,1)}, bf16[128,1024]{1,0:T(8,128)(2,1)S(1)}, u32[]{:S(2)}, u32[]{:S(2)}) collective-permute-start(bf16[128,1024]{1,0:T(8,128)(2,1)} %get-tuple-element.34), channel_id=1, source_target_pairs={{0,24},{8,0},{16,8},{24,16},{1,25},{9,1},{17,9},{25,17},{2,26},{10... | collective-permute-start | bytes 786440 | tf_op jit(solution)/shard_map/ppermute | solution.py:39
  106.2 4.5 %copy-start.4 = (f32[128,1024]{1,0:T(8,128)S(1)}, f32[128,1024]{1,0:T(8,128)}, u32[]{:S(2)}) copy-start(f32[128,1024]{1,0:T(8,128)} %copy-done.3) | copy-start | bytes 1572868
  112.7 50.5 %all-to-all-start.2 = ((bf16[8,128,1024]{2,1,0:T(8,128)(2,1)}), bf16[8,128,1024]{2,1,0:T(8,128)(2,1)}, u32[]{:S(2)}, u32[]{:S(2)}) async-start(bf16[8,128,1024]{2,1,0:T(8,128)(2,1)} %broadcast_in_dim.134), calls=%async_computation.2 | async-start | bytes 4194304 | tf_op jit(solution)/shard_map/all_to_all | solution.py:132
  117.1 79.1 %reduce-scatter.2.cloned.1.call-start = ((), (), s32[]{:S(2)}) async-start(), calls=%async_computation.6 | async-start | bytes 1310720 | tf_op jit(solution)/shard_map/reduce_scatter | solution.py:145
  157.7 4.0 %copy-start = (f32[1024,1024]{1,0:T(8,128)S(1)}, f32[1024,1024]{1,0:T(8,128)}, u32[]{:S(2)}) copy-start(f32[1024,1024]{1,0:T(8,128)} %all-gather.2.cloned.1.call-done) | copy-start | bytes 12582916
  157.7 4.7 %copy-start.2 = (bf16[1024,1024]{1,0:T(8,128)(2,1)S(1)}, bf16[1024,1024]{1,0:T(8,128)(2,1)}, u32[]{:S(2)}) copy-start(bf16[1024,1024]{1,0:T(8,128)(2,1)} %all-reduce.2.cloned.1.call-done) | copy-start | bytes 6291460
  (1 other events, 0.7 us)
Sparse Core Ops, SparseCore 0:
  13.2 39.2 all-gather.1
  88.8 68.7 all-reduce.1
  169.5 26.6 reduce-scatter.1
where the time goes:
time: 205 us
  waiting for transfers between devices  86.3 us (42%)
  matrix products  43.5 us (21%)
  starting transfers between devices  27.8 us (14%)
  other arithmetic  17.9 us (9%)
  local copies, waits for them, and re-layouts  15 us (7%)
  between operations  14 us (7%)
    psum x1, waiting for transfers between devices, body(): code_delta = lax.psum(code_sum, 'member').astype(jnp.float32)  37.8 us
    ppermute x3, waiting for transfers between devices, exchange(): lax.ppermute(sent, axis, [(i, (i + s) % size) for i in range(size)])  16.4 us
    all_gather x1, waiting for transfers between devices, body(): lax.all_gather(jnp.dot(code_feat, projection, preferred_element_type=jnp....  15 us
    reduce_scatter x1, waiting for transfers between devices, body(): lax.psum_scatter(sent_proj, 'group', scatter_dimension=0, tiled=True)  12.3 us
    ppermute x6, starting transfers between devices, shift_all(): lax.ppermute(x, axis, [(i, (i + s) % size) for i in range(size)])  11.5 us
    dot_general x1, matrix products, body(): jnp.einsum('qe,de->qd', dz_query, projection, preferred_element_type=jnp....  7.24 us
    dot_general x1, matrix products, body(): jnp.einsum('qe,de->qd', dz_code, projection, preferred_element_type=jnp.f...  7.24 us
    dot_general x1, matrix products, body(): jnp.dot(code_feat, projection, preferred_element_type=jnp.float32)  5.85 us
  transfers between devices with their start and end apart: 15, of which 8 were waited for; matrix products, arithmetic and copies ran while one was open for 30% of the time, Pallas kernels for 0%

commit v1 on v0

--- a/solution.py
+++ b/solution.py
@@ -113,7 +113,7 @@
         code_terms = term if code_terms is None else code_terms + term
     code_sum = code_terms.astype(jnp.bfloat16)
     grad_dq, code_sum = lax.optimization_barrier((grad, code_sum))
-    code_delta = lax.psum(code_sum, "member").astype(jnp.float32)
+    code_delta = jnp.sum(lax.all_gather(code_sum, "member"), axis=0).astype(jnp.float32)
     delta_parts = jnp.einsum(
         "gqk,ke->gqe", grad_dq, group_codes, preferred_element_type=jnp.float32
     )

time: 205 us -> 260 us (1.27)
  waiting for transfers between devices: 86.3 us -> 133 us
  other arithmetic: 17.9 us -> 26.7 us
    all_to_all x1, waiting for transfers between devices: 0.01 us -> 48.3 us  [body(): lax.all_to_all(jnp.broadcast_to(dz_query[None], (members, queries_dev, em...]
    psum x1 -> x0, waiting for transfers between devices: 37.8 us -> none  [body(): code_delta = lax.psum(code_sum, 'member').astype(jnp.float32)]
    all_gather x0 -> x1, waiting for transfers between devices: none -> 15.8 us  [body(): lax.all_gather(code_sum, 'member')]
    reduce_sum x0 -> x1, other arithmetic: none -> 9.46 us  [body(): jnp.sum(lax.all_gather(code_sum, 'member'), axis=0).astype(jnp.float32)]
    all_to_all x1, waiting for transfers between devices: 0.01 us -> 9.05 us  [body(): lax.all_to_all(feats, 'member', split_axis=0, concat_axis=0, tiled=True)]
    all_gather x1, waiting for transfers between devices: 15 us -> 20.6 us  [body(): lax.all_gather(jnp.dot(code_feat, projection, preferred_element_type=jnp....]
    ppermute x3, waiting for transfers between devices: 16.4 us -> 21.7 us  [exchange(): lax.ppermute(sent, axis, [(i, (i + s) % size) for i in range(size)])]
  transfers between devices with their start and end apart: 15 -> 15, of which waited for: 8 -> 10; matrix products, arithmetic and copies ran while one was open for 30% -> 19% of each run, Pallas kernels for 0% -> 0%
where the time goes in v1:
time: 260 us; the launch traced here: 259 us
  waiting for transfers between devices  133 us (51%)
  matrix products  45.6 us (18%)
  other arithmetic  26.7 us (10%)
  starting transfers between devices  26 us (10%)
  local copies, waits for them, and re-layouts  14.2 us (5%)
  between operations  14.1 us (5%)
    all_to_all x1, waiting for transfers between devices, body(): lax.all_to_all(jnp.broadcast_to(dz_query[None], (members, queries_dev, em...  48.3 us
    ppermute x3, waiting for transfers between devices, exchange(): lax.ppermute(sent, axis, [(i, (i + s) % size) for i in range(size)])  21.7 us
    all_gather x1, waiting for transfers between devices, body(): lax.all_gather(jnp.dot(code_feat, projection, preferred_element_type=jnp....  20.6 us
    all_gather x1, waiting for transfers between devices, body(): lax.all_gather(code_sum, 'member')  15.8 us
    reduce_scatter x1, waiting for transfers between devices, body(): lax.psum_scatter(sent_proj, 'group', scatter_dimension=0, tiled=True)  12.9 us
    ppermute x6, starting transfers between devices, shift_all(): lax.ppermute(x, axis, [(i, (i + s) % size) for i in range(size)])  10.6 us
    reduce_sum x1, other arithmetic, body(): jnp.sum(lax.all_gather(code_sum, 'member'), axis=0).astype(jnp.float32)  9.46 us
    all_to_all x1, waiting for transfers between devices, body(): lax.all_to_all(feats, 'member', split_axis=0, concat_axis=0, tiled=True)  9.05 us
  transfers between devices with their start and end apart: 15, of which 10 were waited for; matrix products, arithmetic and copies ran while one was open for 19% of the time, Pallas kernels for 0%

profile of v1, /device:TPU:0, one launch (start us, length us, event | category | flops | bytes accessed | tf_op | source)
XLA Modules:
  0.0 259.2 jit_solution(13685385001736643720)
XLA Ops:
  7.2 5.8 %fusion.26 = f32[128,1024]{1,0:T(8,128)} fusion(bf16[128,4096]{1,0:T(8,128)(2,1)} %param.10, bf16[4096,1024]{1,0:T(8,128)(2,1)} %param.11), kind=kOutput, calls=%fused_computation.91 | convolution fusion | flops 1073741824 | bytes 9961472 | tf_op jit(solution)/shard_map/dot_general | solution.py:63
  13.1 5.1 %collective-permute-start.2 = (s32[16]{0:T(128)S(1)}, s32[16]{0:T(128)S(1)}, u32[]{:S(2)}, u32[]{:S(2)}) collective-permute-start(s32[16]{0:T(128)S(1)} %bitcast.130), channel_id=1, source_target_pairs={{0,24},{8,0},{16,8},{24,16},{1,25},{9,1},{17,9},{25,17},{2,26},{10... | collective-permute-start | bytes 200 | tf_op jit(solution)/shard_map/ppermute | solution.py:28
  19.2 4.8 %multiply_reduce_fusion.2 = (f32[128]{0:T(128)S(1)}, f32[128,1024]{1,0:T(8,128)S(1)}) fusion(bf16[128,4096]{1,0:T(8,128)(2,1)S(1)} %copy-done.6, bf16[4096,1024]{1,0:T(8,128)(2,1)} %param.11), kind=kOutput, calls=%fused_computation.31 | convolution fusion | flops 1074003840 | bytes 9961984 | tf_op jit(solution)/shard_map/dot_general | solution.py:12
  26.0 4.0 %all-to-all-start = ((bf16[4,128,1024]{2,1,0:T(8,128)(2,1)}), bf16[4,128,1024]{2,1,0:T(8,128)(2,1)S(1)}, u32[]{:S(2)}, u32[]{:S(2)}) async-start(bf16[4,128,1024]{2,1,0:T(8,128)(2,1)} %broadcast_in_dim.126), calls=%async_computation | async-start | bytes 2097152 | tf_op jit(solution)/shard_map/all_to_all | solution.py:71
  32.0 20.6 %all-gather.4.cloned.1.call-done = f32[1024,1024]{1,0:T(8,128)} async-done(((f32[128,1024]{1,0:T(8,128)}), f32[1024,1024]{1,0:T(8,128)}) %all-gather.4.cloned.1.call-update) | async-done | bytes 4194320 | tf_op jit(solution)/shard_map/all_gather | solution.py:62
  52.6 2.5 multiply_reduce_fusion
  55.2 3.6 %fusion.24 = (f32[4,128]{1,0:T(4,128)S(1)}, f32[4,128,1024]{2,1,0:T(8,128)S(1)}) fusion(bf16[4,128,1024]{2,1,0:T(8,128)(2,1)S(1)} %all-to-all-done, f32[1024,1024]{1,0:T(8,128)} %all-gather.4.cloned.1.call-done, f32[1024]{0:T(1024)S(1)} %add_rsqrt_fusion, pred[4,1024]{1,0:T(4,128)(4,1)S(1)} %broadcast_in_dim.124), kind=kOutput, calls=%fused_computation.89 | convolution fusion | flops 1077411328 | bytes 7350272 | tf_op jit(solution)/shard_map/gqe,ke->gqk/dot_general | solution.py:86
  59.5 3.3 %collective-permute-start.5 = (f32[3,4,128]{2,1,0:T(4,128)S(1)}, f32[3,4,128]{2,1,0:T(4,128)S(1)}, u32[]{:S(2)}, u32[]{:S(2)}) collective-permute-start(f32[3,4,128]{2,1,0:T(4,128)S(1)} %get-tuple-element.38), channel_id=1, source_target_pairs={{0,24},{8,0},{16,8},{24,16},{1,25},{9,1},{17,9},{25,17},{2,26},{10... | collective-permute-start | bytes 18440 | tf_op jit(solution)/shard_map/ppermute | solution.py:28
  64.2 3.2 %collective-permute-done.4 = f32[3,4,128]{2,1,0:T(4,128)S(1)} collective-permute-done((f32[3,4,128]{2,1,0:T(4,128)S(1)}, f32[3,4,128]{2,1,0:T(4,128)S(1)}, u32[]{:S(2)}, u32[]{:S(2)}) %collective-permute-start.4) | collective-permute-done | bytes 6176 | tf_op jit(solution)/shard_map/ppermute | solution.py:28
  79.4 3.8 %all-to-all-start.1 = ((bf16[8,2,128,4,128]{2,4,3,1,0:T(8,128)(2,1)}), bf16[8,2,128,4,128]{2,4,3,1,0:T(8,128)(2,1)S(1)}, u32[]{:S(2)}, u32[]{:S(2)}) async-start(bf16[8,2,128,4,128]{2,4,3,1,0:T(8,128)(2,1)} %copy.25), calls=%async_computation.1 | async-start | bytes 4194304 | tf_op jit(solution)/shard_map/all_to_all | solution.py:60
  83.3 5.4 %fusion.25 = (bf16[4,128,1024]{2,1,0:T(8,128)(2,1)S(1)}, f32[4,128,1024]{2,1,0:T(8,128)}) fusion(bf16[4,128,1024]{2,1,0:T(8,128)(2,1)S(1)} %copy-done.3, f32[1024,1024]{1,0:T(8,128)} %all-gather.4.cloned.1.call-done, f32[1024]{0:T(1024)S(1)} %add_rsqrt_fusion), kind=kOutput, calls=%fused_computation.90 | convolution fusion | flops 1076363264 | bytes 8392704 | tf_op jit(solution)/shard_map/gqk,ke->gqe/dot_general | solution.py:117
  91.9 6.8 %collective-permute-done.8 = bf16[128,1024]{1,0:T(8,128)(2,1)S(1)} collective-permute-done((bf16[128,1024]{1,0:T(8,128)(2,1)S(1)}, bf16[128,1024]{1,0:T(8,128)(2,1)S(1)}, u32[]{:S(2)}, u32[]{:S(2)}) %collective-permute-start.8) | collective-permute-done | bytes 262176 | tf_op jit(solution)/shard_map/ppermute | solution.py:39
  98.7 14.9 %collective-permute-done.7 = bf16[128,1024]{1,0:T(8,128)(2,1)S(1)} collective-permute-done((bf16[128,1024]{1,0:T(8,128)(2,1)S(1)}, bf16[128,1024]{1,0:T(8,128)(2,1)S(1)}, u32[]{:S(2)}, u32[]{:S(2)}) %collective-permute-start.7) | collective-permute-done | bytes 262176 | tf_op jit(solution)/shard_map/ppermute | solution.py:39
  114.7 2.9 %gather_fusion.2 = bf16[4,128,1024]{2,1,0:T(8,128)(2,1)} fusion(bf16[4,128,1024]{2,1,0:T(8,128)(2,1)} %pad_maximum_fusion, s32[1024]{0:T(1024)S(1)} %pad_clamp_fusion), kind=kCustom, calls=%fused_computation.2 | custom fusion | bytes 2097168 | tf_op jit(solution)/shard_map/jit(_take)/gather | solution.py:41
  121.6 9.0 %all-to-all-done.1 = bf16[8,2,128,4,128]{2,4,3,1,0:T(8,128)(2,1)S(1)} async-done(((bf16[8,2,128,4,128]{2,4,3,1,0:T(8,128)(2,1)}), bf16[8,2,128,4,128]{2,4,3,1,0:T(8,128)(2,1)S(1)}, u32[]{:S(2)}, u32[]{:S(2)}) %all-to-all-start.1) | async-done | bytes 2097184 | tf_op jit(solution)/shard_map/all_to_all | solution.py:60
  132.3 4.5 %all-to-all-start.2 = ((bf16[8,128,1024]{2,1,0:T(8,128)(2,1)}), bf16[8,128,1024]{2,1,0:T(8,128)(2,1)}, u32[]{:S(2)}, u32[]{:S(2)}) async-start(bf16[8,128,1024]{2,1,0:T(8,128)(2,1)} %broadcast_in_dim.134), calls=%async_computation.2 | async-start | bytes 4194304 | tf_op jit(solution)/shard_map/all_to_all | solution.py:132
  138.0 48.3 %all-to-all-done.2 = bf16[8,128,1024]{2,1,0:T(8,128)(2,1)} async-done(((bf16[8,128,1024]{2,1,0:T(8,128)(2,1)}), bf16[8,128,1024]{2,1,0:T(8,128)(2,1)}, u32[]{:S(2)}, u32[]{:S(2)}) %all-to-all-start.2) | async-done | bytes 2097184 | tf_op jit(solution)/shard_map/all_to_all | solution.py:132
  186.3 4.5 %fusion.4 = f32[4,128,1024,1]{2,1,3,0:T(8,128)} fusion(bf16[8,128,1024]{2,1,0:T(8,128)(2,1)} %all-to-all-done.2, bf16[8,1,128,4,128]{2,4,3,1,0:T(8,128)(2,1)} %get-tuple-element.32), kind=kOutput, calls=%fused_computation.16 | convolution fusion | flops 1073741824 | bytes 5242880 | tf_op jit(solution)/shard_map/mqgr,mqe->gre/dot_general | solution.py:140
  190.8 15.8 %all-gather.6.cloned.1.call-done = bf16[8192,1024]{1,0:T(8,128)(2,1)} async-done(((bf16[1024,1024]{1,0:T(8,128)(2,1)}), bf16[8192,1024]{1,0:T(8,128)(2,1)}) %all-gather.6.cloned.1.call-update) | async-done | bytes 16777232 | tf_op jit(solution)/shard_map/all_gather | solution.py:116
  206.6 9.5 %reduce_sum.81 = bf16[1024,1024]{1,0:T(8,128)(2,1)S(1)} reduce(bf16[8,1024,1024]{2,1,0:T(8,128)(2,1)} %bitcast.117, bf16[]{:T(256)} %constant.131.clone.1), dimensions={0}, to_apply=%region_9.12 | reduce | flops 7340032 | bytes 18874370 | tf_op jit(solution)/shard_map/reduce_sum | solution.py:116
  216.1 3.0 %fusion = f32[1024]{0:T(1024)S(1)} fusion(bf16[1024,1024]{1,0:T(8,128)(2,1)S(1)} %reduce_sum.81, f32[1024,1024]{1,0:T(8,128)} %all-gather.4.cloned.1.call-done, f32[1024]{0:T(1024)S(1)} %add_rsqrt_fusion), kind=kLoop, calls=%fused_computation.7 | loop fusion | flops 4193280 | bytes 6299648 | tf_op jit(solution)/shard_map/reduce_sum | solution.py:19
  223.4 7.2 %convolution_convert_fusion.1 = bf16[128,4096]{1,0:T(8,128)(2,1)} fusion(bf16[128,1024]{1,0:T(8,128)(2,1)S(1)} %multiply_convert_fusion.2, bf16[4096,1024]{1,0:T(8,128)(2,1)} %param.11), kind=kOutput, calls=%fused_computation.6 | convolution fusion | flops 1074266112 | bytes 9699328 | tf_op jit(solution)/shard_map/qe,de->qd/dot_general | solution.py:126
  230.7 7.3 %convolution_convert_fusion = bf16[128,4096]{1,0:T(8,128)(2,1)} fusion(bf16[4096,1024]{1,0:T(8,128)(2,1)} %param.11, bf16[1024,1024]{1,0:T(8,128)(2,1)} %copy-done.1, s32[]{:T(128)S(6)} %select_n.153), kind=kOutput, calls=%fused_computation.5 | convolution fusion | flops 1074266112 | bytes 9699332 | tf_op jit(solution)/shard_map/qe,de->qd/dot_general | solution.py:129
  238.0 12.9 %reduce-scatter.2.cloned.1.call-done = bf16[1,128,1024]{2,1,0:T(8,128)(2,1)} async-done(((bf16[4,128,1024]{2,1,0:T(8,128)(2,1)}), bf16[1,128,1024]{2,1,0:T(8,128)(2,1)}) %reduce-scatter.2.cloned.1.call-update) | async-done | bytes 262160 | tf_op jit(solution)/shard_map/reduce_scatter | solution.py:145
  (93 shorter events, 36.3 us)
Async XLA Ops:
  7.2 5.9 %copy-start.11 = (s32[1,16]{1,0:T(1,128)S(1)}, s32[1,16]{1,0:T(1,128)}, u32[]{:S(2)}) copy-start(s32[1,16]{1,0:T(1,128)} %param.12) | copy-start | bytes 196
  7.2 12.1 %copy-start.6 = (bf16[128,4096]{1,0:T(8,128)(2,1)S(1)}, bf16[128,4096]{1,0:T(8,128)(2,1)}, u32[]{:S(2)}) copy-start(bf16[128,4096]{1,0:T(8,128)(2,1)} %param.9) | copy-start | bytes 3145732
  7.2 45.4 %all-gather.4.cloned.1.call-start = ((), (), s32[]{:S(2)}) async-start(), calls=%async_computation.4 | async-start | bytes 4718592 | tf_op jit(solution)/shard_map/all_gather | solution.py:62
  13.1 17.9 %collective-permute-start.2 = (s32[16]{0:T(128)S(1)}, s32[16]{0:T(128)S(1)}, u32[]{:S(2)}, u32[]{:S(2)}) collective-permute-start(s32[16]{0:T(128)S(1)} %bitcast.130), channel_id=1, source_target_pairs={{0,24},{8,0},{16,8},{24,16},{1,25},{9,1},{17,9},{25,17},{2,26},{10... | collective-permute-start | bytes 200 | tf_op jit(solution)/shard_map/ppermute | solution.py:28
  18.2 12.8 %collective-permute-start.1 = (s32[16]{0:T(128)S(1)}, s32[16]{0:T(128)S(1)}, u32[]{:S(2)}, u32[]{:S(2)}) collective-permute-start(s32[16]{0:T(128)S(1)} %bitcast.131), channel_id=1, source_target_pairs={{0,16},{8,24},{16,0},{24,8},{1,17},{9,25},{17,1},{25,9},{2,18},{10... | collective-permute-start | bytes 200 | tf_op jit(solution)/shard_map/ppermute | solution.py:28
  18.2 12.8 %collective-permute-start = (s32[16]{0:T(128)S(1)}, s32[16]{0:T(128)S(1)}, u32[]{:S(2)}, u32[]{:S(2)}) collective-permute-start(s32[16]{0:T(128)S(1)} %bitcast.132), channel_id=1, source_target_pairs={{0,8},{8,16},{16,24},{24,0},{1,9},{9,17},{17,25},{25,1},{2,10},{10... | collective-permute-start | bytes 200 | tf_op jit(solution)/shard_map/ppermute | solution.py:28
  26.0 29.2 %all-to-all-start = ((bf16[4,128,1024]{2,1,0:T(8,128)(2,1)}), bf16[4,128,1024]{2,1,0:T(8,128)(2,1)S(1)}, u32[]{:S(2)}, u32[]{:S(2)}) async-start(bf16[4,128,1024]{2,1,0:T(8,128)(2,1)} %broadcast_in_dim.126), calls=%async_computation | async-start | bytes 2097152 | tf_op jit(solution)/shard_map/all_to_all | solution.py:71
  30.0 176.6 %all-gather.6.cloned.1.call-start = ((), (), s32[]{:S(2)}) async-start(), calls=%async_computation.6 | async-start | bytes 18874368 | tf_op jit(solution)/shard_map/all_gather | solution.py:116
  59.5 4.7 %collective-permute-start.5 = (f32[3,4,128]{2,1,0:T(4,128)S(1)}, f32[3,4,128]{2,1,0:T(4,128)S(1)}, u32[]{:S(2)}, u32[]{:S(2)}) collective-permute-start(f32[3,4,128]{2,1,0:T(4,128)S(1)} %get-tuple-element.38), channel_id=1, source_target_pairs={{0,24},{8,0},{16,8},{24,16},{1,25},{9,1},{17,9},{25,17},{2,26},{10... | collective-permute-start | bytes 18440 | tf_op jit(solution)/shard_map/ppermute | solution.py:28
  62.9 4.5 %collective-permute-start.4 = (f32[3,4,128]{2,1,0:T(4,128)S(1)}, f32[3,4,128]{2,1,0:T(4,128)S(1)}, u32[]{:S(2)}, u32[]{:S(2)}) collective-permute-start(f32[3,4,128]{2,1,0:T(4,128)S(1)} %get-tuple-element.38), channel_id=1, source_target_pairs={{0,16},{8,24},{16,0},{24,8},{1,17},{9,25},{17,1},{25,9},{2,18},{10... | collective-permute-start | bytes 18440 | tf_op jit(solution)/shard_map/ppermute | solution.py:28
  62.9 5.4 %collective-permute-start.3 = (f32[3,4,128]{2,1,0:T(4,128)S(1)}, f32[3,4,128]{2,1,0:T(4,128)S(1)}, u32[]{:S(2)}, u32[]{:S(2)}) collective-permute-start(f32[3,4,128]{2,1,0:T(4,128)S(1)} %get-tuple-element.38), channel_id=1, source_target_pairs={{0,8},{8,16},{16,24},{24,0},{1,9},{9,17},{17,25},{25,1},{2,10},{10... | collective-permute-start | bytes 18440 | tf_op jit(solution)/shard_map/ppermute | solution.py:28
  70.6 2.2 copy-start.2
  75.2 1.9 copy-start.7
  79.4 3.9 %copy-start.3 = (bf16[4,128,1024]{2,1,0:T(8,128)(2,1)S(1)}, bf16[4,128,1024]{2,1,0:T(8,128)(2,1)}, u32[]{:S(2)}) copy-start(bf16[4,128,1024]{2,1,0:T(8,128)(2,1)} %copy-done.2) | copy-start | bytes 3145732
  79.4 51.3 %all-to-all-start.1 = ((bf16[8,2,128,4,128]{2,4,3,1,0:T(8,128)(2,1)}), bf16[8,2,128,4,128]{2,4,3,1,0:T(8,128)(2,1)S(1)}, u32[]{:S(2)}, u32[]{:S(2)}) async-start(bf16[8,2,128,4,128]{2,4,3,1,0:T(8,128)(2,1)} %copy.25), calls=%async_computation.1 | async-start | bytes 4194304 | tf_op jit(solution)/shard_map/all_to_all | solution.py:60
  88.8 9.9 %collective-permute-start.8 = (bf16[128,1024]{1,0:T(8,128)(2,1)S(1)}, bf16[128,1024]{1,0:T(8,128)(2,1)S(1)}, u32[]{:S(2)}, u32[]{:S(2)}) collective-permute-start(bf16[128,1024]{1,0:T(8,128)(2,1)S(1)} %get-tuple-element.34), channel_id=1, source_target_pairs={{0,24},{8,0},{16,8},{24,16},{1,25},{9,1},{17,9},{25,17},{2,26},{10... | collective-permute-start | bytes 786440 | tf_op jit(solution)/shard_map/ppermute | solution.py:39
  89.6 24.0 %collective-permute-start.7 = (bf16[128,1024]{1,0:T(8,128)(2,1)S(1)}, bf16[128,1024]{1,0:T(8,128)(2,1)S(1)}, u32[]{:S(2)}, u32[]{:S(2)}) collective-permute-start(bf16[128,1024]{1,0:T(8,128)(2,1)S(1)} %get-tuple-element.35), channel_id=1, source_target_pairs={{0,16},{8,24},{16,0},{24,8},{1,17},{9,25},{17,1},{25,9},{2,18},{10... | collective-permute-start | bytes 786440 | tf_op jit(solution)/shard_map/ppermute | solution.py:39
  89.9 23.6 %collective-permute-start.6 = (bf16[128,1024]{1,0:T(8,128)(2,1)S(1)}, bf16[128,1024]{1,0:T(8,128)(2,1)S(1)}, u32[]{:S(2)}, u32[]{:S(2)}) collective-permute-start(bf16[128,1024]{1,0:T(8,128)(2,1)S(1)} %get-tuple-element.36), channel_id=1, source_target_pairs={{0,8},{8,16},{16,24},{24,0},{1,9},{9,17},{17,25},{25,1},{2,10},{10... | collective-permute-start | bytes 786440 | tf_op jit(solution)/shard_map/ppermute | solution.py:39
  114.7 4.5 %copy-start.5 = (f32[128,1024]{1,0:T(8,128)S(1)}, f32[128,1024]{1,0:T(8,128)}, u32[]{:S(2)}) copy-start(f32[128,1024]{1,0:T(8,128)} %copy-done.4) | copy-start | bytes 1572868
  132.3 53.9 %all-to-all-start.2 = ((bf16[8,128,1024]{2,1,0:T(8,128)(2,1)}), bf16[8,128,1024]{2,1,0:T(8,128)(2,1)}, u32[]{:S(2)}, u32[]{:S(2)}) async-start(bf16[8,128,1024]{2,1,0:T(8,128)(2,1)} %broadcast_in_dim.134), calls=%async_computation.2 | async-start | bytes 4194304 | tf_op jit(solution)/shard_map/all_to_all | solution.py:132
  136.8 114.1 %reduce-scatter.2.cloned.1.call-start = ((), (), s32[]{:S(2)}) async-start(), calls=%async_computation.5 | async-start | bytes 1310720 | tf_op jit(solution)/shard_map/reduce_scatter | solution.py:145
  216.1 3.5 %copy-start = (f32[1024,1024]{1,0:T(8,128)S(1)}, f32[1024,1024]{1,0:T(8,128)}, u32[]{:S(2)}) copy-start(f32[1024,1024]{1,0:T(8,128)} %all-gather.4.cloned.1.call-done) | copy-start | bytes 12582916
  219.5 1.6 copy-start.9
  220.4 3.0 %copy-start.1 = (bf16[1024,1024]{1,0:T(8,128)(2,1)}, bf16[1024,1024]{1,0:T(8,128)(2,1)S(1)}, u32[]{:S(2)}) copy-start(bf16[1024,1024]{1,0:T(8,128)(2,1)S(1)} %fusion.2) | copy-start | bytes 6291460
  (3 other events, 2.7 us)
Sparse Core Ops, SparseCore 0:
  13.2 39.3 all-gather.3
  75.3 131.2 all-gather.5
  223.5 27.2 reduce-scatter.1
